TPU v7x, 512 devices: a whole 4x8x8 slice. The times are simulated.
512 devices in a mesh: seq: 128 (over z, y_hi, x, core), head: 4 (over y_lo).
Axes of the slice: x: 4, y: 8 (y_hi: 2, y_lo: 4; y = y_hi * 4 + y_lo), z: 8, core: 2. Of those that a mesh axis runs over, the one named last changes fastest.
Arguments:
- query_rows: bfloat16 [32768, 8, 128], P('seq', 'head'), may hold values from -20 to 20
- key_rows: bfloat16 [32768, 8, 128], P('seq', 'head'), may hold values from -20 to 20
- value_rows: bfloat16 [32768, 8, 128], P('seq', 'head'), may hold values from -6 to 6
- cotangent: bfloat16 [32768, 8, 128], P('seq', 'head'), may hold values from -6 to 6
- norm_gain: float32 [8, 128], P('head'), may hold values from 0.5 to 2
- offsets: int32 [8], P('head'), may hold values from 0 to 31, as said below
Outputs:
- query_grad: bfloat16 [32768, 8, 128], P('seq', 'head')
- key_grad: bfloat16 [32768, 8, 128], P('seq', 'head')
- value_grad: bfloat16 [32768, 8, 128], P('seq', 'head')
Inputs may be any that keep to these rules, and one draw needn't show every extreme that they name: The heads' offsets are distinct.
All inputs are finite; a program needn't handle non-finite values.
Results may differ from a plain program's by a relative error of at most 0.018.
Values may be sent and summed in bfloat16 or wider, within the bound.
No kernel may reach another device: no remote copies, remote signals or barrier semaphores. Data moves between devices by JAX's collectives and lax.ppermute only.
A program may use at most 128 MiB of HBM per device.

v0:
```python
import numpy as np
import jax
import jax.numpy as jnp
from jax import lax
from jax.sharding import PartitionSpec as P

RATE2 = 4
RATE3 = 16
RATE4 = 32
RATES = (1, RATE2, RATE3, RATE4)
neg_fill = -1e30
epsilon = 1e-05
lane = 128


def pick_rows(source, wanted, stride):
    row_count = source.shape[0] // stride
    shaped = source.reshape((row_count, stride) + source.shape[1:])
    trailing = (1,) * (source.ndim - 2)
    target = wanted.reshape((1, 1, -1) + trailing)
    column = jnp.arange(stride, dtype=jnp.int32).reshape((1, stride, 1) + trailing)
    zeroed = jnp.where(column == target, shaped, jnp.zeros((), source.dtype))
    return jnp.sum(zeroed, axis=1, dtype=source.dtype)


def put_rows(compact, wanted, stride, filler):
    trailing = (1,) * (compact.ndim - 2)
    target = wanted.reshape((1, 1, -1) + trailing)
    column = jnp.arange(stride, dtype=jnp.int32).reshape((1, stride, 1) + trailing)
    spread = jnp.where(column == target, compact[:, None], jnp.asarray(filler, compact.dtype))
    return spread.reshape((compact.shape[0] * stride,) + compact.shape[1:])


def exchange_order(count):
    bits = [1 << bit for bit in range(max(0, (count - 1).bit_length()))]
    order = []
    for first in range(0, len(bits), 2):
        order.extend(reversed(bits[first : first + 2]))
    return order


def spread(order, slots):
    table = np.zeros(slots, np.int32)
    for slot in range(slots):
        for bit, offset in enumerate(order):
            if slot >> bit & 1:
                table[slot] ^= offset
    return table


def extend(parts, spans, order, toward):
    count = lax.axis_size("seq")
    live = sorted(range(len(parts)), key=lambda index: -spans[index])
    sizes = [part.shape[0] for part in parts]
    state = jnp.concatenate([parts[index] for index in live], axis=0)[None]
    finished = {}
    for offset in order + [None]:
        while live and spans[live[-1]] <= state.shape[0]:
            index = live.pop()
            start = sum((sizes[other] for other in live))
            finished[index] = state[:, start : start + sizes[index]]
            state = state[:, :start]
        if not live:
            break
        pairs = [(source, source ^ offset) for source in range(count)]
        if all((spans[index] <= 2 * state.shape[0] for index in live)):
            pairs = [pair for pair in pairs if (pair[1] > pair[0]) == (toward > 0)]
        moved = lax.ppermute(state, "seq", pairs)
        state = jnp.concatenate([state, moved], axis=0)
    return [finished[index] for index in range(len(parts))]


def split_exact(value):
    high = lax.reduce_precision(value, exponent_bits=8, mantissa_bits=7)
    rest = value - high
    middle = lax.reduce_precision(rest, exponent_bits=8, mantissa_bits=7)
    low = rest - middle
    return jnp.stack([high, middle, low]).astype(jnp.bfloat16)


def stats_rows(rows, heads_dev):
    return -(-(rows * heads_dev * 6) // (16 * lane)) * 16


def pack_stats(lse_sel, delta_sel):
    rows, heads_dev = lse_sel.shape
    coded = split_exact(jnp.stack([lse_sel.T, delta_sel.T])).reshape(-1)
    padded = stats_rows(rows, heads_dev) * lane
    coded = jnp.pad(coded, (0, padded - coded.shape[0]))
    return coded.reshape(padded // lane, lane)


def unpack_stats(coded, slots, rows, heads_dev):
    width = 2 * heads_dev * rows
    parts = coded.reshape(slots, -1)[:, : 3 * width].reshape(slots, 3, width)
    parts = parts.astype(jnp.float32)
    values = parts[:, 0] + parts[:, 1] + parts[:, 2]
    values = values.reshape(slots, 2, heads_dev, rows).transpose(1, 2, 0, 3)
    values = values.reshape(2, heads_dev, slots * rows)
    return (values[0], values[1])


def shards(query_rows, key_rows, value_rows, cotangent, norm_gain, offsets):
    tok_dev, heads_dev, head_size = query_rows.shape
    seq_count = lax.axis_size("seq")
    device = lax.axis_index("seq")
    group_rows = tok_dev * seq_count // RATE4
    score_scale = head_size ** (-0.5)
    features = heads_dev * head_size * lax.axis_size("head")
    levels = []
    for stride in RATES:
        span = max(1, stride * group_rows // tok_dev)
        rows = tok_dev // stride
        wanted = offsets % stride
        levels.append(
            dict(
                stride=stride,
                span=span,
                rows=rows,
                wanted=wanted,
                spot=device % span,
                key_sel=pick_rows(key_rows, wanted, stride),
                value_sel=pick_rows(value_rows, wanted, stride),
                query_sel=pick_rows(query_rows, wanted, stride),
            )
        )
    spans = [level["span"] for level in levels]
    order = exchange_order(seq_count)
    for level in levels:
        level["owner"] = level["spot"] ^ jnp.asarray(spread(order, level["span"]))
    key_sets = extend(
        [
            jnp.concatenate(
                [level["key_sel"].reshape(-1, lane), level["value_sel"].reshape(-1, lane)], axis=0
            )
            for level in levels
        ],
        spans,
        order,
        1,
    )
    query_sets = extend(
        [level["query_sel"].reshape(-1, lane) for level in levels], spans, order, -1
    )
    lse_total = jnp.full((tok_dev, heads_dev), neg_fill, jnp.float32)
    for level, key_set in zip(levels, key_sets):
        span, rows = (level["span"], level["rows"])
        paired = key_set.reshape(span, 2, rows, heads_dev, head_size)
        keys = paired[:, 0].reshape(span * rows, heads_dev, head_size)
        level["key_all"] = keys
        level["value_all"] = paired[:, 1].reshape(span * rows, heads_dev, head_size)
        raw = (
            jnp.einsum("qhd,khd->hqk", level["query_sel"], keys, preferred_element_type=jnp.float32)
            * score_scale
        )
        key_at = (
            level["owner"][:, None] * rows + jnp.arange(rows, dtype=jnp.int32)[None, :]
        ).reshape(1, span * rows)
        query_at = (level["spot"] * rows + jnp.arange(rows, dtype=jnp.int32))[:, None]
        linked = key_at <= query_at
        scores = jnp.where(linked[None], raw, neg_fill)
        row_peak = jnp.max(scores, axis=2)
        level_lse = row_peak + jnp.log(jnp.sum(jnp.exp(scores - row_peak[:, :, None]), axis=2))
        level["scores"] = scores
        lse_total = jnp.logaddexp(
            lse_total, put_rows(level_lse.T, level["wanted"], level["stride"], neg_fill)
        )
    attended = jnp.zeros((tok_dev, heads_dev, head_size), jnp.float32)
    for level in levels:
        lse_sel = pick_rows(lse_total, level["wanted"], level["stride"])
        weights = jnp.exp(level["scores"] - lse_sel.T[:, :, None])
        level["lse_sel"] = lse_sel
        level["weights"] = weights
        out_sel = jnp.einsum(
            "hqk,khd->qhd",
            weights.astype(jnp.bfloat16),
            level["value_all"],
            preferred_element_type=jnp.float32,
        )
        attended = attended + put_rows(out_sel, level["wanted"], level["stride"], 0.0)
    grad_in = cotangent.astype(jnp.float32) * norm_gain[None]
    sums = lax.psum(
        jnp.stack(
            [
                jnp.sum(attended, axis=(1, 2)),
                jnp.sum(attended * attended, axis=(1, 2)),
                jnp.sum(grad_in, axis=(1, 2)),
                jnp.sum(grad_in * attended, axis=(1, 2)),
            ]
        ),
        "head",
    )
    centre = sums[0] / features
    variance = sums[1] / features - centre * centre
    inverse = lax.rsqrt(variance + epsilon)
    first_mean = sums[2] / features
    second_mean = inverse * (sums[3] / features - centre * first_mean)
    normed = (attended - centre[:, None, None]) * inverse[:, None, None]
    d_attended = (
        inverse[:, None, None]
        * (grad_in - first_mean[:, None, None] - normed * second_mean[:, None, None])
    ).astype(jnp.bfloat16)
    row_delta = jnp.sum(d_attended.astype(jnp.float32) * attended, axis=2)
    query_grad = jnp.zeros((tok_dev, heads_dev, head_size), jnp.float32)
    back_sets = []
    for level in levels:
        dout_sel = pick_rows(d_attended, level["wanted"], level["stride"])
        delta_sel = pick_rows(row_delta, level["wanted"], level["stride"])
        back_sets.append(
            jnp.concatenate(
                [dout_sel.reshape(-1, lane), pack_stats(level["lse_sel"], delta_sel)], axis=0
            )
        )
        weight_grad = jnp.einsum(
            "qhd,khd->hqk", dout_sel, level["value_all"], preferred_element_type=jnp.float32
        )
        score_grad = (level["weights"] * (weight_grad - delta_sel.T[:, :, None])).astype(
            jnp.bfloat16
        )
        grad_sel = jnp.einsum(
            "hqk,khd->qhd", score_grad, level["key_all"], preferred_element_type=jnp.float32
        )
        query_grad = query_grad + put_rows(
            grad_sel * score_scale, level["wanted"], level["stride"], 0.0
        )
    back_sets = extend(back_sets, spans, order, -1)
    key_grad = jnp.zeros((tok_dev, heads_dev, head_size), jnp.float32)
    value_grad = jnp.zeros((tok_dev, heads_dev, head_size), jnp.float32)
    for level, query_set, back_set in zip(levels, query_sets, back_sets):
        span, rows = (level["span"], level["rows"])
        queries = query_set.reshape(span * rows, heads_dev, head_size)
        back_slots = back_set.reshape(span, -1, lane)
        dout_all = back_slots[:, : rows * heads_dev].reshape(span * rows, heads_dev, head_size)
        lse_all, delta_all = unpack_stats(back_slots[:, rows * heads_dev :], span, rows, heads_dev)
        raw = (
            jnp.einsum(
                "qhd,khd->hqk", queries, level["key_sel"], preferred_element_type=jnp.float32
            )
            * score_scale
        )
        query_at = (
            level["owner"][:, None] * rows + jnp.arange(rows, dtype=jnp.int32)[None, :]
        ).reshape(span * rows, 1)
        key_at = (level["spot"] * rows + jnp.arange(rows, dtype=jnp.int32))[None, :]
        linked = query_at >= key_at
        scores = jnp.where(linked[None], raw, neg_fill)
        weights = jnp.exp(scores - lse_all[:, :, None])
        value_grad_sel = jnp.einsum(
            "hqk,qhd->khd",
            weights.astype(jnp.bfloat16),
            dout_all,
            preferred_element_type=jnp.float32,
        )
        weight_grad = jnp.einsum(
            "qhd,khd->hqk", dout_all, level["value_sel"], preferred_element_type=jnp.float32
        )
        score_grad = (weights * (weight_grad - delta_all[:, :, None])).astype(jnp.bfloat16)
        key_grad_sel = jnp.einsum(
            "hqk,qhd->khd", score_grad, queries, preferred_element_type=jnp.float32
        )
        key_grad = key_grad + put_rows(
            key_grad_sel * score_scale, level["wanted"], level["stride"], 0.0
        )
        value_grad = value_grad + put_rows(value_grad_sel, level["wanted"], level["stride"], 0.0)
    return (
        query_grad.astype(jnp.bfloat16),
        key_grad.astype(jnp.bfloat16),
        value_grad.astype(jnp.bfloat16),
    )


def solution(mesh):
    placed = (
        P("seq", "head", None),
        P("seq", "head", None),
        P("seq", "head", None),
        P("seq", "head", None),
        P("head", None),
        P("head"),
    )
    return jax.shard_map(
        shards,
        mesh=mesh,
        in_specs=placed,
        out_specs=(P("seq", "head", None), P("seq", "head", None), P("seq", "head", None)),
        check_vma=False,
    )
```

profile of v0, /device:TPU:74, one launch (start us, length us, event | category | flops | bytes accessed | tf_op | source)
XLA Modules:
  0.0 368.6 jit_solution(18264421656202876044)
XLA Ops:
  10.6 3.5 collective-permute-start.7
  19.5 4.2 %collective-permute-done.7 = bf16[1,688,128]{2,1,0:T(8,128)(2,1)S(1)} collective-permute-done((bf16[1,688,128]{2,1,0:T(8,128)(2,1)S(1)}, bf16[1,688,128]{2,1,0:T(8,128)(2,1)S(1)}, u32[]{:S(2)}, u32[]{:S(2)}) %collective-permute-start.7) | collective-permute-done | bytes 176160 | tf_op jit(solution)/shard_map/ppermute | solution.py:68
  29.7 6.8 %collective-permute-start.11 = (bf16[4,176,128]{2,1,0:T(8,128)(2,1)S(1)}, bf16[4,176,128]{2,1,0:T(8,128)(2,1)S(1)}, u32[]{:S(2)}, u32[]{:S(2)}) collective-permute-start(bf16[4,176,128]{2,1,0:T(8,128)(2,1)S(1)} %pad_maximum_fusion.31), channel_id=1, source_target_pairs={{0,32},{4,36},{8,40},{12,44},{16,48},{20,52},{24,56},{28,60},{32,0... | collective-permute-start | bytes 540680 | tf_op jit(solution)/shard_map/ppermute | solution.py:68
  44.7 4.0 %collective-permute-start.12 = (bf16[8,176,128]{2,1,0:T(8,128)(2,1)S(1)}, bf16[8,176,128]{2,1,0:T(8,128)(2,1)S(1)}, u32[]{:S(2)}, u32[]{:S(2)}) collective-permute-start(bf16[8,176,128]{2,1,0:T(8,128)(2,1)S(1)} %pad_maximum_fusion.24), channel_id=1, source_target_pairs={{0,16},{4,20},{8,24},{12,28},{16,0},{20,4},{24,8},{28,12},{32,48},... | collective-permute-start | bytes 1081352 | tf_op jit(solution)/shard_map/ppermute | solution.py:68
  49.0 7.0 %collective-permute-start.2 = (bf16[4,352,128]{2,1,0:T(8,128)(2,1)S(1)}, bf16[4,352,128]{2,1,0:T(8,128)(2,1)S(1)}, u32[]{:S(2)}, u32[]{:S(2)}) collective-permute-start(bf16[4,352,128]{2,1,0:T(8,128)(2,1)S(1)} %pad_maximum_fusion.23), channel_id=1, source_target_pairs={{0,32},{4,36},{8,40},{12,44},{16,48},{20,52},{24,56},{28,60},{32,0... | collective-permute-start | bytes 1081352 | tf_op jit(solution)/shard_map/ppermute | solution.py:68
  58.4 6.1 %collective-permute-start.15 = (bf16[16,48,128]{2,1,0:T(8,128)(2,1)S(1)}, bf16[16,48,128]{2,1,0:T(8,128)(2,1)S(1)}, u32[]{:S(2)}, u32[]{:S(2)}) collective-permute-start(bf16[16,48,128]{2,1,0:T(8,128)(2,1)S(1)} %pad_maximum_fusion.30), channel_id=1, source_target_pairs={{0,128},{4,132},{8,136},{12,140},{16,144},{20,148},{24,152},{28,15... | collective-permute-start | bytes 589832 | tf_op jit(solution)/shard_map/ppermute | solution.py:68
  66.5 3.7 %collective-permute-done.15 = bf16[16,48,128]{2,1,0:T(8,128)(2,1)S(1)} collective-permute-done((bf16[16,48,128]{2,1,0:T(8,128)(2,1)S(1)}, bf16[16,48,128]{2,1,0:T(8,128)(2,1)S(1)}, u32[]{:S(2)}, u32[]{:S(2)}) %collective-permute-start.15) | collective-permute-done | bytes 196640 | tf_op jit(solution)/shard_map/ppermute | solution.py:68
  73.6 4.0 %collective-permute-start.3 = (bf16[8,352,128]{2,1,0:T(8,128)(2,1)S(1)}, bf16[8,352,128]{2,1,0:T(8,128)(2,1)S(1)}, u32[]{:S(2)}, u32[]{:S(2)}) collective-permute-start(bf16[8,352,128]{2,1,0:T(8,128)(2,1)S(1)} %pad_maximum_fusion.8), channel_id=1, source_target_pairs={{0,16},{4,20},{8,24},{12,28},{16,0},{20,4},{24,8},{28,12},{32,48},... | collective-permute-start | bytes 2162696 | tf_op jit(solution)/shard_map/ppermute | solution.py:68
  84.9 8.1 %collective-permute-done.3 = bf16[8,352,128]{2,1,0:T(8,128)(2,1)S(1)} collective-permute-done((bf16[8,352,128]{2,1,0:T(8,128)(2,1)S(1)}, bf16[8,352,128]{2,1,0:T(8,128)(2,1)S(1)}, u32[]{:S(2)}, u32[]{:S(2)}) %collective-permute-start.3) | collective-permute-done | bytes 720928 | tf_op jit(solution)/shard_map/ppermute | solution.py:68
  93.1 5.3 %collective-permute-start.4 = (bf16[16,96,128]{2,1,0:T(8,128)(2,1)S(1)}, bf16[16,96,128]{2,1,0:T(8,128)(2,1)S(1)}, u32[]{:S(2)}, u32[]{:S(2)}) collective-permute-start(bf16[16,96,128]{2,1,0:T(8,128)(2,1)S(1)} %pad_maximum_fusion.20), channel_id=1, source_target_pairs={{0,128},{4,132},{8,136},{12,140},{16,144},{20,148},{24,152},{28,15... | collective-permute-start | bytes 1179656 | tf_op jit(solution)/shard_map/ppermute | solution.py:68
  103.9 14.1 %collective-permute-done.4 = bf16[16,96,128]{2,1,0:T(8,128)(2,1)S(1)} collective-permute-done((bf16[16,96,128]{2,1,0:T(8,128)(2,1)S(1)}, bf16[16,96,128]{2,1,0:T(8,128)(2,1)S(1)}, u32[]{:S(2)}, u32[]{:S(2)}) %collective-permute-start.4) | collective-permute-done | bytes 393248 | tf_op jit(solution)/shard_map/ppermute | solution.py:68
  128.6 12.0 %collective-permute-done.5 = bf16[32,96,128]{2,1,0:T(8,128)(2,1)} collective-permute-done((bf16[32,96,128]{2,1,0:T(8,128)(2,1)}, bf16[32,96,128]{2,1,0:T(8,128)(2,1)}, u32[]{:S(2)}, u32[]{:S(2)}) %collective-permute-start.5) | collective-permute-done | bytes 786464 | tf_op jit(solution)/shard_map/ppermute | solution.py:68
  142.5 6.3 %collective-permute-start.6 = (bf16[64,32,128]{2,1,0:T(8,128)(2,1)}, bf16[64,32,128]{2,1,0:T(8,128)(2,1)}, u32[]{:S(2)}, u32[]{:S(2)}) collective-permute-start(bf16[64,32,128]{2,1,0:T(8,128)(2,1)} %pad_maximum_fusion.17), channel_id=1, source_target_pairs={{0,256},{4,260},{8,264},{12,268},{16,272},{20,276},{24,280},{28,28... | collective-permute-start | bytes 1572872 | tf_op jit(solution)/shard_map/ppermute | solution.py:68
  156.5 13.8 %collective-permute-done.6 = bf16[64,32,128]{2,1,0:T(8,128)(2,1)} collective-permute-done((bf16[64,32,128]{2,1,0:T(8,128)(2,1)}, bf16[64,32,128]{2,1,0:T(8,128)(2,1)}, u32[]{:S(2)}, u32[]{:S(2)}) %collective-permute-start.6) | collective-permute-done | bytes 524320 | tf_op jit(solution)/shard_map/ppermute | solution.py:68
  193.4 13.3 %psum.7 = f32[4,256]{1,0:T(4,128)S(1)} all-reduce(f32[4,256]{1,0:T(4,128)S(1)} %pad_maximum_fusion.34), channel_id=1, replica_groups=mesh['seq'=128,'head'=4] {'head'}, use_global_device_ids=true, to_apply=%region_24.25 | all-reduce | flops 1024 | bytes 8192 | tf_op jit(solution)/shard_map/psum | solution.py:182
  226.6 3.5 collective-permute-done.9
  247.6 4.1 %collective-permute-start.13 = (bf16[4,224,128]{2,1,0:T(8,128)(2,1)S(1)}, bf16[4,224,128]{2,1,0:T(8,128)(2,1)S(1)}, u32[]{:S(2)}, u32[]{:S(2)}) collective-permute-start(bf16[4,224,128]{2,1,0:T(8,128)(2,1)S(1)} %pad_maximum_fusion.29), channel_id=1, source_target_pairs={{0,32},{4,36},{8,40},{12,44},{16,48},{20,52},{24,56},{28,60},{32,0... | collective-permute-start | bytes 688136 | tf_op jit(solution)/shard_map/ppermute | solution.py:68
  253.4 12.9 %collective-permute-done.13 = bf16[4,224,128]{2,1,0:T(8,128)(2,1)S(1)} collective-permute-done((bf16[4,224,128]{2,1,0:T(8,128)(2,1)S(1)}, bf16[4,224,128]{2,1,0:T(8,128)(2,1)S(1)}, u32[]{:S(2)}, u32[]{:S(2)}) %collective-permute-start.13) | collective-permute-done | bytes 229408 | tf_op jit(solution)/shard_map/ppermute | solution.py:68
  266.4 4.0 %collective-permute-start.14 = (bf16[8,224,128]{2,1,0:T(8,128)(2,1)S(1)}, bf16[8,224,128]{2,1,0:T(8,128)(2,1)S(1)}, u32[]{:S(2)}, u32[]{:S(2)}) collective-permute-start(bf16[8,224,128]{2,1,0:T(8,128)(2,1)S(1)} %pad_maximum_fusion.19), channel_id=1, source_target_pairs={{0,16},{4,20},{8,24},{12,28},{16,0},{20,4},{24,8},{28,12},{32,48},... | collective-permute-start | bytes 1376264 | tf_op jit(solution)/shard_map/ppermute | solution.py:68
  272.9 9.3 %collective-permute-done.14 = bf16[8,224,128]{2,1,0:T(8,128)(2,1)S(1)} collective-permute-done((bf16[8,224,128]{2,1,0:T(8,128)(2,1)S(1)}, bf16[8,224,128]{2,1,0:T(8,128)(2,1)S(1)}, u32[]{:S(2)}, u32[]{:S(2)}) %collective-permute-start.14) | collective-permute-done | bytes 458784 | tf_op jit(solution)/shard_map/ppermute | solution.py:68
  287.6 10.1 %collective-permute-done.17 = bf16[16,80,128]{2,1,0:T(8,128)(2,1)} collective-permute-done((bf16[16,80,128]{2,1,0:T(8,128)(2,1)S(1)}, bf16[16,80,128]{2,1,0:T(8,128)(2,1)}, u32[]{:S(2)}, u32[]{:S(2)}) %collective-permute-start.17) | collective-permute-done | bytes 327712 | tf_op jit(solution)/shard_map/ppermute | solution.py:68
  299.6 4.1 %collective-permute-start.18 = (bf16[32,80,128]{2,1,0:T(8,128)(2,1)}, bf16[32,80,128]{2,1,0:T(8,128)(2,1)}, u32[]{:S(2)}, u32[]{:S(2)}) collective-permute-start(bf16[32,80,128]{2,1,0:T(8,128)(2,1)} %pad_maximum_fusion.12), channel_id=1, source_target_pairs={{0,64},{4,68},{8,72},{12,76},{16,80},{20,84},{24,88},{28,92},{32,9... | collective-permute-start | bytes 1966088 | tf_op jit(solution)/shard_map/ppermute | solution.py:68
  313.7 4.1 %collective-permute-done.18 = bf16[32,80,128]{2,1,0:T(8,128)(2,1)} collective-permute-done((bf16[32,80,128]{2,1,0:T(8,128)(2,1)}, bf16[32,80,128]{2,1,0:T(8,128)(2,1)}, u32[]{:S(2)}, u32[]{:S(2)}) %collective-permute-start.18) | collective-permute-done | bytes 655392 | tf_op jit(solution)/shard_map/ppermute | solution.py:68
  332.1 17.7 %collective-permute-done.20 = bf16[64,32,128]{2,1,0:T(8,128)(2,1)} collective-permute-done((bf16[64,32,128]{2,1,0:T(8,128)(2,1)}, bf16[64,32,128]{2,1,0:T(8,128)(2,1)}, u32[]{:S(2)}, u32[]{:S(2)}) %collective-permute-start.20) | collective-permute-done | bytes 524320 | tf_op jit(solution)/shard_map/ppermute | solution.py:68
  (468 shorter events, 184.1 us)
Async XLA Ops:
  1.5 35.7 %copy-start.76 = (pred[32,2]{0,1:T(4,128)(4,1)}, pred[32,2]{0,1:T(4,128)(4,1)S(1)}, u32[]{:S(2)}) copy-start(pred[32,2]{0,1:T(4,128)(4,1)S(1)} %iota_compare_fusion.2) | copy-start | bytes 196
  8.0 17.6 %collective-permute-start = (bf16[1,1376,128]{2,1,0:T(8,128)(2,1)S(1)}, bf16[1,1376,128]{2,1,0:T(8,128)(2,1)S(1)}, u32[]{:S(2)}, u32[]{:S(2)}) collective-permute-start(bf16[1,1376,128]{2,1,0:T(8,128)(2,1)S(1)} %bitcast.328), channel_id=1, source_target_pairs={{0,8},{4,12},{8,0},{12,4},{16,24},{20,28},{24,16},{28,20},{32,40},... | collective-permute-start | bytes 1056776 | tf_op jit(solution)/shard_map/ppermute | solution.py:68
  10.6 13.1 %collective-permute-start.7 = (bf16[1,688,128]{2,1,0:T(8,128)(2,1)S(1)}, bf16[1,688,128]{2,1,0:T(8,128)(2,1)S(1)}, u32[]{:S(2)}, u32[]{:S(2)}) collective-permute-start(bf16[1,688,128]{2,1,0:T(8,128)(2,1)S(1)} %maximum_bitcast_fusion), channel_id=1, source_target_pairs={{0,8},{4,12},{8,0},{12,4},{16,24},{20,28},{24,16},{28,20},{32,40},... | collective-permute-start | bytes 528392 | tf_op jit(solution)/shard_map/ppermute | solution.py:68
  23.7 6.0 %collective-permute-start.8 = (bf16[2,688,128]{2,1,0:T(8,128)(2,1)S(1)}, bf16[2,688,128]{2,1,0:T(8,128)(2,1)S(1)}, u32[]{:S(2)}, u32[]{:S(2)}) collective-permute-start(bf16[2,688,128]{2,1,0:T(8,128)(2,1)S(1)} %pad_maximum_fusion.25), channel_id=1, source_target_pairs={{0,4},{4,0},{8,12},{12,8},{16,20},{20,16},{24,28},{28,24},{32,36},... | collective-permute-start | bytes 1056776 | tf_op jit(solution)/shard_map/ppermute | solution.py:68
  26.6 22.2 %collective-permute-start.1 = (bf16[2,1376,128]{2,1,0:T(8,128)(2,1)}, bf16[2,1376,128]{2,1,0:T(8,128)(2,1)S(1)}, u32[]{:S(2)}, u32[]{:S(2)}) collective-permute-start(bf16[2,1376,128]{2,1,0:T(8,128)(2,1)} %pad_maximum_fusion.10), channel_id=1, source_target_pairs={{0,4},{4,0},{8,12},{12,8},{16,20},{20,16},{24,28},{28,24},{32,36},... | collective-permute-start | bytes 2113544 | tf_op jit(solution)/shard_map/ppermute | solution.py:68
  29.7 15.0 %collective-permute-start.11 = (bf16[4,176,128]{2,1,0:T(8,128)(2,1)S(1)}, bf16[4,176,128]{2,1,0:T(8,128)(2,1)S(1)}, u32[]{:S(2)}, u32[]{:S(2)}) collective-permute-start(bf16[4,176,128]{2,1,0:T(8,128)(2,1)S(1)} %pad_maximum_fusion.31), channel_id=1, source_target_pairs={{0,32},{4,36},{8,40},{12,44},{16,48},{20,52},{24,56},{28,60},{32,0... | collective-permute-start | bytes 540680 | tf_op jit(solution)/shard_map/ppermute | solution.py:68
  38.0 205.0 %copy-start.46 = (pred[256,2]{0,1:T(4,128)(4,1)}, pred[256,2]{0,1:T(4,128)(4,1)S(1)}, u32[]{:S(2)}) copy-start(pred[256,2]{0,1:T(4,128)(4,1)S(1)} %broadcast_in_dim.631) | copy-start | bytes 1540
  38.8 152.3 %copy-start.48 = (pred[256,2]{0,1:T(4,128)(4,1)}, pred[256,2]{0,1:T(4,128)(4,1)S(1)}, u32[]{:S(2)}) copy-start(pred[256,2]{0,1:T(4,128)(4,1)S(1)} %broadcast_in_dim.625) | copy-start | bytes 1540
  44.7 12.8 %collective-permute-start.12 = (bf16[8,176,128]{2,1,0:T(8,128)(2,1)S(1)}, bf16[8,176,128]{2,1,0:T(8,128)(2,1)S(1)}, u32[]{:S(2)}, u32[]{:S(2)}) collective-permute-start(bf16[8,176,128]{2,1,0:T(8,128)(2,1)S(1)} %pad_maximum_fusion.24), channel_id=1, source_target_pairs={{0,16},{4,20},{8,24},{12,28},{16,0},{20,4},{24,8},{28,12},{32,48},... | collective-permute-start | bytes 1081352 | tf_op jit(solution)/shard_map/ppermute | solution.py:68
  49.0 24.5 %collective-permute-start.2 = (bf16[4,352,128]{2,1,0:T(8,128)(2,1)S(1)}, bf16[4,352,128]{2,1,0:T(8,128)(2,1)S(1)}, u32[]{:S(2)}, u32[]{:S(2)}) collective-permute-start(bf16[4,352,128]{2,1,0:T(8,128)(2,1)S(1)} %pad_maximum_fusion.23), channel_id=1, source_target_pairs={{0,32},{4,36},{8,40},{12,44},{16,48},{20,52},{24,56},{28,60},{32,0... | collective-permute-start | bytes 1081352 | tf_op jit(solution)/shard_map/ppermute | solution.py:68
  58.4 11.9 %collective-permute-start.15 = (bf16[16,48,128]{2,1,0:T(8,128)(2,1)S(1)}, bf16[16,48,128]{2,1,0:T(8,128)(2,1)S(1)}, u32[]{:S(2)}, u32[]{:S(2)}) collective-permute-start(bf16[16,48,128]{2,1,0:T(8,128)(2,1)S(1)} %pad_maximum_fusion.30), channel_id=1, source_target_pairs={{0,128},{4,132},{8,136},{12,140},{16,144},{20,148},{24,152},{28,15... | collective-permute-start | bytes 589832 | tf_op jit(solution)/shard_map/ppermute | solution.py:68
  70.3 12.2 %collective-permute-start.16 = (bf16[32,48,128]{2,1,0:T(8,128)(2,1)S(1)}, bf16[32,48,128]{2,1,0:T(8,128)(2,1)S(1)}, u32[]{:S(2)}, u32[]{:S(2)}) collective-permute-start(bf16[32,48,128]{2,1,0:T(8,128)(2,1)S(1)} %pad_maximum_fusion.22), channel_id=1, source_target_pairs={{0,64},{4,68},{8,72},{12,76},{16,80},{20,84},{24,88},{28,92},{32,9... | collective-permute-start | bytes 1179656 | tf_op jit(solution)/shard_map/ppermute | solution.py:68
  73.6 19.4 %collective-permute-start.3 = (bf16[8,352,128]{2,1,0:T(8,128)(2,1)S(1)}, bf16[8,352,128]{2,1,0:T(8,128)(2,1)S(1)}, u32[]{:S(2)}, u32[]{:S(2)}) collective-permute-start(bf16[8,352,128]{2,1,0:T(8,128)(2,1)S(1)} %pad_maximum_fusion.8), channel_id=1, source_target_pairs={{0,16},{4,20},{8,24},{12,28},{16,0},{20,4},{24,8},{28,12},{32,48},... | collective-permute-start | bytes 2162696 | tf_op jit(solution)/shard_map/ppermute | solution.py:68
  82.5 19.5 %collective-permute-start.19 = (bf16[64,16,128]{2,1,0:T(8,128)(2,1)S(1)}, bf16[64,16,128]{2,1,0:T(8,128)(2,1)S(1)}, u32[]{:S(2)}, u32[]{:S(2)}) collective-permute-start(bf16[64,16,128]{2,1,0:T(8,128)(2,1)S(1)} %pad_maximum_fusion.27), channel_id=1, source_target_pairs={{256,0},{260,4},{264,8},{268,12},{272,16},{276,20},{280,24},{284,2... | collective-permute-start | bytes 786440 | tf_op jit(solution)/shard_map/ppermute | solution.py:68
  93.1 24.9 %collective-permute-start.4 = (bf16[16,96,128]{2,1,0:T(8,128)(2,1)S(1)}, bf16[16,96,128]{2,1,0:T(8,128)(2,1)S(1)}, u32[]{:S(2)}, u32[]{:S(2)}) collective-permute-start(bf16[16,96,128]{2,1,0:T(8,128)(2,1)S(1)} %pad_maximum_fusion.20), channel_id=1, source_target_pairs={{0,128},{4,132},{8,136},{12,140},{16,144},{20,148},{24,152},{28,15... | collective-permute-start | bytes 1179656 | tf_op jit(solution)/shard_map/ppermute | solution.py:68
  119.0 21.7 %collective-permute-start.5 = (bf16[32,96,128]{2,1,0:T(8,128)(2,1)}, bf16[32,96,128]{2,1,0:T(8,128)(2,1)}, u32[]{:S(2)}, u32[]{:S(2)}) collective-permute-start(bf16[32,96,128]{2,1,0:T(8,128)(2,1)} %pad_maximum_fusion.5), channel_id=1, source_target_pairs={{0,64},{4,68},{8,72},{12,76},{16,80},{20,84},{24,88},{28,92},{32,9... | collective-permute-start | bytes 2359304 | tf_op jit(solution)/shard_map/ppermute | solution.py:68
  142.5 27.8 %collective-permute-start.6 = (bf16[64,32,128]{2,1,0:T(8,128)(2,1)}, bf16[64,32,128]{2,1,0:T(8,128)(2,1)}, u32[]{:S(2)}, u32[]{:S(2)}) collective-permute-start(bf16[64,32,128]{2,1,0:T(8,128)(2,1)} %pad_maximum_fusion.17), channel_id=1, source_target_pairs={{0,256},{4,260},{8,264},{12,268},{16,272},{20,276},{24,280},{28,28... | collective-permute-start | bytes 1572872 | tf_op jit(solution)/shard_map/ppermute | solution.py:68
  222.5 7.6 %collective-permute-start.9 = (bf16[1,768,128]{2,1,0:T(8,128)(2,1)S(1)}, bf16[1,768,128]{2,1,0:T(8,128)(2,1)S(1)}, u32[]{:S(2)}, u32[]{:S(2)}) collective-permute-start(bf16[1,768,128]{2,1,0:T(8,128)(2,1)S(1)} %bitcast.332), channel_id=1, source_target_pairs={{0,8},{4,12},{8,0},{12,4},{16,24},{20,28},{24,16},{28,20},{32,40},... | collective-permute-start | bytes 589832 | tf_op jit(solution)/shard_map/ppermute | solution.py:68
  231.5 14.4 %collective-permute-start.10 = (bf16[2,768,128]{2,1,0:T(8,128)(2,1)}, bf16[2,768,128]{2,1,0:T(8,128)(2,1)S(1)}, u32[]{:S(2)}, u32[]{:S(2)}) collective-permute-start(bf16[2,768,128]{2,1,0:T(8,128)(2,1)} %pad_maximum_fusion.21), channel_id=1, source_target_pairs={{0,4},{4,0},{8,12},{12,8},{16,20},{20,16},{24,28},{28,24},{32,36},... | collective-permute-start | bytes 1179656 | tf_op jit(solution)/shard_map/ppermute | solution.py:68
  247.6 18.7 %collective-permute-start.13 = (bf16[4,224,128]{2,1,0:T(8,128)(2,1)S(1)}, bf16[4,224,128]{2,1,0:T(8,128)(2,1)S(1)}, u32[]{:S(2)}, u32[]{:S(2)}) collective-permute-start(bf16[4,224,128]{2,1,0:T(8,128)(2,1)S(1)} %pad_maximum_fusion.29), channel_id=1, source_target_pairs={{0,32},{4,36},{8,40},{12,44},{16,48},{20,52},{24,56},{28,60},{32,0... | collective-permute-start | bytes 688136 | tf_op jit(solution)/shard_map/ppermute | solution.py:68
  266.4 15.8 %collective-permute-start.14 = (bf16[8,224,128]{2,1,0:T(8,128)(2,1)S(1)}, bf16[8,224,128]{2,1,0:T(8,128)(2,1)S(1)}, u32[]{:S(2)}, u32[]{:S(2)}) collective-permute-start(bf16[8,224,128]{2,1,0:T(8,128)(2,1)S(1)} %pad_maximum_fusion.19), channel_id=1, source_target_pairs={{0,16},{4,20},{8,24},{12,28},{16,0},{20,4},{24,8},{28,12},{32,48},... | collective-permute-start | bytes 1376264 | tf_op jit(solution)/shard_map/ppermute | solution.py:68
  282.2 15.5 %collective-permute-start.17 = (bf16[16,80,128]{2,1,0:T(8,128)(2,1)S(1)}, bf16[16,80,128]{2,1,0:T(8,128)(2,1)}, u32[]{:S(2)}, u32[]{:S(2)}) collective-permute-start(bf16[16,80,128]{2,1,0:T(8,128)(2,1)S(1)} %pad_maximum_fusion.26), channel_id=1, source_target_pairs={{0,128},{4,132},{8,136},{12,140},{16,144},{20,148},{24,152},{28,15... | collective-permute-start | bytes 983048 | tf_op jit(solution)/shard_map/ppermute | solution.py:68
  299.6 18.2 %collective-permute-start.18 = (bf16[32,80,128]{2,1,0:T(8,128)(2,1)}, bf16[32,80,128]{2,1,0:T(8,128)(2,1)}, u32[]{:S(2)}, u32[]{:S(2)}) collective-permute-start(bf16[32,80,128]{2,1,0:T(8,128)(2,1)} %pad_maximum_fusion.12), channel_id=1, source_target_pairs={{0,64},{4,68},{8,72},{12,76},{16,80},{20,84},{24,88},{28,92},{32,9... | collective-permute-start | bytes 1966088 | tf_op jit(solution)/shard_map/ppermute | solution.py:68
  319.8 30.0 %collective-permute-start.20 = (bf16[64,32,128]{2,1,0:T(8,128)(2,1)}, bf16[64,32,128]{2,1,0:T(8,128)(2,1)}, u32[]{:S(2)}, u32[]{:S(2)}) collective-permute-start(bf16[64,32,128]{2,1,0:T(8,128)(2,1)} %get-tuple-element.33), channel_id=1, source_target_pairs={{256,0},{260,4},{264,8},{268,12},{272,16},{276,20},{280,24},{284,2... | collective-permute-start | bytes 1572872 | tf_op jit(solution)/shard_map/ppermute | solution.py:68
  (87 other events, 948.7 us)
where the time goes:
time: 371 us; the launch traced here: 369 us
  waiting for transfers between devices  123 us (33%)
  starting transfers between devices  76.5 us (21%)
  local copies, waits for them, and re-layouts  70 us (19%)
  other arithmetic  46.2 us (12%)
  matrix products  37.5 us (10%)
  blocking collectives  13.3 us (4%)
    ppermute x21, waiting for transfers between devices, extend(): moved = lax.ppermute(state, 'seq', pairs)  123 us
    ppermute x21, starting transfers between devices, extend(): moved = lax.ppermute(state, 'seq', pairs)  76.5 us
    broadcast_in_dim x45, local copies, waits for them, and re-layouts, put_rows(): jnp.where(column == target, compact[:, None], jnp.asarray(filler, compact...  30.1 us
    psum x1, blocking collectives, shards(): lax.psum(jnp.stack([jnp.sum(attended, axis=(1, 2)), jnp.sum(attended * at...  13.3 us
    concatenate x20, other arithmetic, extend(): state = jnp.concatenate([state, moved], axis=0)  13.2 us
    unnamed x205, local copies, waits for them, and re-layouts  12.9 us
    reduce_sum x12, other arithmetic, pick_rows(): return jnp.sum(zeroed, axis=1, dtype=source.dtype)  12.1 us
    dot_general x4, matrix products, shards(): jnp.einsum('hqk,qhd->khd', score_grad, queries, preferred_element_type=jn...  8.41 us
  transfers between devices with their start and end apart: 21, of which 16 were waited for; matrix products, arithmetic and copies ran while one was open for 21% of the time, Pallas kernels for 0%

commit v1 on v0

--- a/solution.py
+++ b/solution.py
@@ -11,6 +11,12 @@
 neg_fill = -1e30
 epsilon = 1e-05
 lane = 128
+
+
+def _link_meshes(x_local):
+    carry_out = lax.all_gather(x_local, "head")
+    aux = jnp.sum(carry_out, 0)
+    return aux
 
 
 def pick_rows(source, wanted, stride):
@@ -179,7 +185,7 @@
         )
         attended = attended + put_rows(out_sel, level["wanted"], level["stride"], 0.0)
     grad_in = cotangent.astype(jnp.float32) * norm_gain[None]
-    sums = lax.psum(
+    sums = _link_meshes(
         jnp.stack(
             [
                 jnp.sum(attended, axis=(1, 2)),
@@ -187,8 +193,7 @@
                 jnp.sum(grad_in, axis=(1, 2)),
                 jnp.sum(grad_in * attended, axis=(1, 2)),
             ]
-        ),
-        "head",
+        )
     )
     centre = sums[0] / features
     variance = sums[1] / features - centre * centre

time: 371 us -> 375 us (1.011)
  the two profiles are of different devices: /device:TPU:74 before, /device:TPU:68 now
where the time goes in v1:
time: 375 us; the launch traced here: 372 us
  waiting for transfers between devices  113 us (30%)
  starting transfers between devices  79 us (21%)
  local copies, waits for them, and re-layouts  69.4 us (19%)
  other arithmetic  46.2 us (12%)
  matrix products  37.5 us (10%)
  blocking collectives  24.8 us (7%)
    ppermute x21, waiting for transfers between devices, extend(): moved = lax.ppermute(state, 'seq', pairs)  113 us
    ppermute x21, starting transfers between devices, extend(): moved = lax.ppermute(state, 'seq', pairs)  79 us
    broadcast_in_dim x45, local copies, waits for them, and re-layouts, put_rows(): jnp.where(column == target, compact[:, None], jnp.asarray(filler, compact...  30.1 us
    all_gather x1, blocking collectives, _link_meshes(): carry_out = lax.all_gather(x_local, 'head')  24.8 us
    concatenate x20, other arithmetic, extend(): state = jnp.concatenate([state, moved], axis=0)  13.2 us
    unnamed x205, local copies, waits for them, and re-layouts  12.3 us
    reduce_sum x12, other arithmetic, pick_rows(): return jnp.sum(zeroed, axis=1, dtype=source.dtype)  12.1 us
    dot_general x4, matrix products, shards(): jnp.einsum('hqk,qhd->khd', score_grad, queries, preferred_element_type=jn...  8.4 us
  transfers between devices with their start and end apart: 21, of which 15 were waited for; matrix products, arithmetic and copies ran while one was open for 21% of the time, Pallas kernels for 0%

profile of v1, /device:TPU:68, one launch (start us, length us, event | category | flops | bytes accessed | tf_op | source)
XLA Modules:
  0.0 372.2 jit_solution(11523083052807177934)
XLA Ops:
  8.0 3.1 collective-permute-start
  11.2 2.9 collective-permute-start.7
  19.5 4.2 %collective-permute-done.7 = bf16[1,688,128]{2,1,0:T(8,128)(2,1)S(1)} collective-permute-done((bf16[1,688,128]{2,1,0:T(8,128)(2,1)S(1)}, bf16[1,688,128]{2,1,0:T(8,128)(2,1)S(1)}, u32[]{:S(2)}, u32[]{:S(2)}) %collective-permute-start.7) | collective-permute-done | bytes 176160 | tf_op jit(solution)/shard_map/ppermute | solution.py:74
  29.7 7.7 %collective-permute-start.11 = (bf16[4,176,128]{2,1,0:T(8,128)(2,1)S(1)}, bf16[4,176,128]{2,1,0:T(8,128)(2,1)S(1)}, u32[]{:S(2)}, u32[]{:S(2)}) collective-permute-start(bf16[4,176,128]{2,1,0:T(8,128)(2,1)S(1)} %pad_maximum_fusion.31), channel_id=1, source_target_pairs={{0,32},{4,36},{8,40},{12,44},{16,48},{20,52},{24,56},{28,60},{32,0... | collective-permute-start | bytes 540680 | tf_op jit(solution)/shard_map/ppermute | solution.py:74
  48.0 8.3 %collective-permute-start.2 = (bf16[4,352,128]{2,1,0:T(8,128)(2,1)S(1)}, bf16[4,352,128]{2,1,0:T(8,128)(2,1)S(1)}, u32[]{:S(2)}, u32[]{:S(2)}) collective-permute-start(bf16[4,352,128]{2,1,0:T(8,128)(2,1)S(1)} %pad_maximum_fusion.23), channel_id=1, source_target_pairs={{0,32},{4,36},{8,40},{12,44},{16,48},{20,52},{24,56},{28,60},{32,0... | collective-permute-start | bytes 1081352 | tf_op jit(solution)/shard_map/ppermute | solution.py:74
  57.4 6.1 %collective-permute-start.15 = (bf16[16,48,128]{2,1,0:T(8,128)(2,1)S(1)}, bf16[16,48,128]{2,1,0:T(8,128)(2,1)S(1)}, u32[]{:S(2)}, u32[]{:S(2)}) collective-permute-start(bf16[16,48,128]{2,1,0:T(8,128)(2,1)S(1)} %pad_maximum_fusion.30), channel_id=1, source_target_pairs={{0,128},{4,132},{8,136},{12,140},{16,144},{20,148},{24,152},{28,15... | collective-permute-start | bytes 589832 | tf_op jit(solution)/shard_map/ppermute | solution.py:74
  67.9 3.6 collective-permute-start.16
  71.7 4.0 %collective-permute-start.3 = (bf16[8,352,128]{2,1,0:T(8,128)(2,1)S(1)}, bf16[8,352,128]{2,1,0:T(8,128)(2,1)S(1)}, u32[]{:S(2)}, u32[]{:S(2)}) collective-permute-start(bf16[8,352,128]{2,1,0:T(8,128)(2,1)S(1)} %pad_maximum_fusion.8), channel_id=1, source_target_pairs={{0,16},{4,20},{8,24},{12,28},{16,0},{20,4},{24,8},{28,12},{32,48},... | collective-permute-start | bytes 2162696 | tf_op jit(solution)/shard_map/ppermute | solution.py:74
  80.5 8.8 %collective-permute-done.3 = bf16[8,352,128]{2,1,0:T(8,128)(2,1)S(1)} collective-permute-done((bf16[8,352,128]{2,1,0:T(8,128)(2,1)S(1)}, bf16[8,352,128]{2,1,0:T(8,128)(2,1)S(1)}, u32[]{:S(2)}, u32[]{:S(2)}) %collective-permute-start.3) | collective-permute-done | bytes 720928 | tf_op jit(solution)/shard_map/ppermute | solution.py:74
  89.4 3.2 collective-permute-start.4
  97.2 11.2 %collective-permute-done.4 = bf16[16,96,128]{2,1,0:T(8,128)(2,1)S(1)} collective-permute-done((bf16[16,96,128]{2,1,0:T(8,128)(2,1)S(1)}, bf16[16,96,128]{2,1,0:T(8,128)(2,1)S(1)}, u32[]{:S(2)}, u32[]{:S(2)}) %collective-permute-start.4) | collective-permute-done | bytes 393248 | tf_op jit(solution)/shard_map/ppermute | solution.py:74
  109.4 4.2 %collective-permute-start.5 = (bf16[32,96,128]{2,1,0:T(8,128)(2,1)}, bf16[32,96,128]{2,1,0:T(8,128)(2,1)}, u32[]{:S(2)}, u32[]{:S(2)}) collective-permute-start(bf16[32,96,128]{2,1,0:T(8,128)(2,1)} %pad_maximum_fusion.5), channel_id=1, source_target_pairs={{0,64},{4,68},{8,72},{12,76},{16,80},{20,84},{24,88},{28,92},{32,9... | collective-permute-start | bytes 2359304 | tf_op jit(solution)/shard_map/ppermute | solution.py:74
  121.1 10.1 %collective-permute-done.5 = bf16[32,96,128]{2,1,0:T(8,128)(2,1)} collective-permute-done((bf16[32,96,128]{2,1,0:T(8,128)(2,1)}, bf16[32,96,128]{2,1,0:T(8,128)(2,1)}, u32[]{:S(2)}, u32[]{:S(2)}) %collective-permute-start.5) | collective-permute-done | bytes 786464 | tf_op jit(solution)/shard_map/ppermute | solution.py:74
  133.0 8.8 %collective-permute-start.6 = (bf16[64,32,128]{2,1,0:T(8,128)(2,1)}, bf16[64,32,128]{2,1,0:T(8,128)(2,1)}, u32[]{:S(2)}, u32[]{:S(2)}) collective-permute-start(bf16[64,32,128]{2,1,0:T(8,128)(2,1)} %pad_maximum_fusion.17), channel_id=1, source_target_pairs={{0,256},{4,260},{8,264},{12,268},{16,272},{20,276},{24,280},{28,28... | collective-permute-start | bytes 1572872 | tf_op jit(solution)/shard_map/ppermute | solution.py:74
  149.6 13.5 %collective-permute-done.6 = bf16[64,32,128]{2,1,0:T(8,128)(2,1)} collective-permute-done((bf16[64,32,128]{2,1,0:T(8,128)(2,1)}, bf16[64,32,128]{2,1,0:T(8,128)(2,1)}, u32[]{:S(2)}, u32[]{:S(2)}) %collective-permute-start.6) | collective-permute-done | bytes 524320 | tf_op jit(solution)/shard_map/ppermute | solution.py:74
  185.7 24.8 %all-gather.1 = f32[4,4,256]{2,1,0:T(4,128)S(1)} all-gather(f32[1,4,256]{2,1,0:T(4,128)S(1)} %maximum_bitcast_fusion.2), channel_id=2, replica_groups=mesh['seq'=128,'head'=4] {'head'}, dimensions={0}, use_global_device_ids=true | all-gather | bytes 20480 | tf_op jit(solution)/shard_map/all_gather | solution.py:17
  226.3 3.1 collective-permute-start.9
  251.4 4.1 %collective-permute-start.13 = (bf16[4,224,128]{2,1,0:T(8,128)(2,1)S(1)}, bf16[4,224,128]{2,1,0:T(8,128)(2,1)S(1)}, u32[]{:S(2)}, u32[]{:S(2)}) collective-permute-start(bf16[4,224,128]{2,1,0:T(8,128)(2,1)S(1)} %pad_maximum_fusion.29), channel_id=1, source_target_pairs={{0,32},{4,36},{8,40},{12,44},{16,48},{20,52},{24,56},{28,60},{32,0... | collective-permute-start | bytes 688136 | tf_op jit(solution)/shard_map/ppermute | solution.py:74
  257.2 12.8 %collective-permute-done.13 = bf16[4,224,128]{2,1,0:T(8,128)(2,1)S(1)} collective-permute-done((bf16[4,224,128]{2,1,0:T(8,128)(2,1)S(1)}, bf16[4,224,128]{2,1,0:T(8,128)(2,1)S(1)}, u32[]{:S(2)}, u32[]{:S(2)}) %collective-permute-start.13) | collective-permute-done | bytes 229408 | tf_op jit(solution)/shard_map/ppermute | solution.py:74
  274.9 10.9 %collective-permute-done.14 = bf16[8,224,128]{2,1,0:T(8,128)(2,1)S(1)} collective-permute-done((bf16[8,224,128]{2,1,0:T(8,128)(2,1)S(1)}, bf16[8,224,128]{2,1,0:T(8,128)(2,1)S(1)}, u32[]{:S(2)}, u32[]{:S(2)}) %collective-permute-start.14) | collective-permute-done | bytes 458784 | tf_op jit(solution)/shard_map/ppermute | solution.py:74
  291.3 10.1 %collective-permute-done.17 = bf16[16,80,128]{2,1,0:T(8,128)(2,1)} collective-permute-done((bf16[16,80,128]{2,1,0:T(8,128)(2,1)S(1)}, bf16[16,80,128]{2,1,0:T(8,128)(2,1)}, u32[]{:S(2)}, u32[]{:S(2)}) %collective-permute-start.17) | collective-permute-done | bytes 327712 | tf_op jit(solution)/shard_map/ppermute | solution.py:74
  303.3 4.1 %collective-permute-start.18 = (bf16[32,80,128]{2,1,0:T(8,128)(2,1)}, bf16[32,80,128]{2,1,0:T(8,128)(2,1)}, u32[]{:S(2)}, u32[]{:S(2)}) collective-permute-start(bf16[32,80,128]{2,1,0:T(8,128)(2,1)} %pad_maximum_fusion.12), channel_id=1, source_target_pairs={{0,64},{4,68},{8,72},{12,76},{16,80},{20,84},{24,88},{28,92},{32,9... | collective-permute-start | bytes 1966088 | tf_op jit(solution)/shard_map/ppermute | solution.py:74
  317.5 4.1 %collective-permute-done.18 = bf16[32,80,128]{2,1,0:T(8,128)(2,1)} collective-permute-done((bf16[32,80,128]{2,1,0:T(8,128)(2,1)}, bf16[32,80,128]{2,1,0:T(8,128)(2,1)}, u32[]{:S(2)}, u32[]{:S(2)}) %collective-permute-start.18) | collective-permute-done | bytes 655392 | tf_op jit(solution)/shard_map/ppermute | solution.py:74
  335.9 17.6 %collective-permute-done.20 = bf16[64,32,128]{2,1,0:T(8,128)(2,1)} collective-permute-done((bf16[64,32,128]{2,1,0:T(8,128)(2,1)}, bf16[64,32,128]{2,1,0:T(8,128)(2,1)}, u32[]{:S(2)}, u32[]{:S(2)}) %collective-permute-start.20) | collective-permute-done | bytes 524320 | tf_op jit(solution)/shard_map/ppermute | solution.py:74
  (469 shorter events, 178.5 us)
Async XLA Ops:
  1.5 36.6 %copy-start.76 = (pred[32,2]{0,1:T(4,128)(4,1)}, pred[32,2]{0,1:T(4,128)(4,1)S(1)}, u32[]{:S(2)}) copy-start(pred[32,2]{0,1:T(4,128)(4,1)S(1)} %iota_compare_fusion.2) | copy-start | bytes 196
  8.0 17.6 %collective-permute-start = (bf16[1,1376,128]{2,1,0:T(8,128)(2,1)S(1)}, bf16[1,1376,128]{2,1,0:T(8,128)(2,1)S(1)}, u32[]{:S(2)}, u32[]{:S(2)}) collective-permute-start(bf16[1,1376,128]{2,1,0:T(8,128)(2,1)S(1)} %bitcast.330), channel_id=1, source_target_pairs={{0,8},{4,12},{8,0},{12,4},{16,24},{20,28},{24,16},{28,20},{32,40},... | collective-permute-start | bytes 1056776 | tf_op jit(solution)/shard_map/ppermute | solution.py:74
  11.2 12.4 %collective-permute-start.7 = (bf16[1,688,128]{2,1,0:T(8,128)(2,1)S(1)}, bf16[1,688,128]{2,1,0:T(8,128)(2,1)S(1)}, u32[]{:S(2)}, u32[]{:S(2)}) collective-permute-start(bf16[1,688,128]{2,1,0:T(8,128)(2,1)S(1)} %maximum_bitcast_fusion), channel_id=1, source_target_pairs={{0,8},{4,12},{8,0},{12,4},{16,24},{20,28},{24,16},{28,20},{32,40},... | collective-permute-start | bytes 528392 | tf_op jit(solution)/shard_map/ppermute | solution.py:74
  23.7 6.0 %collective-permute-start.8 = (bf16[2,688,128]{2,1,0:T(8,128)(2,1)S(1)}, bf16[2,688,128]{2,1,0:T(8,128)(2,1)S(1)}, u32[]{:S(2)}, u32[]{:S(2)}) collective-permute-start(bf16[2,688,128]{2,1,0:T(8,128)(2,1)S(1)} %pad_maximum_fusion.25), channel_id=1, source_target_pairs={{0,4},{4,0},{8,12},{12,8},{16,20},{20,16},{24,28},{28,24},{32,36},... | collective-permute-start | bytes 1056776 | tf_op jit(solution)/shard_map/ppermute | solution.py:74
  26.6 21.1 %collective-permute-start.1 = (bf16[2,1376,128]{2,1,0:T(8,128)(2,1)}, bf16[2,1376,128]{2,1,0:T(8,128)(2,1)S(1)}, u32[]{:S(2)}, u32[]{:S(2)}) collective-permute-start(bf16[2,1376,128]{2,1,0:T(8,128)(2,1)} %pad_maximum_fusion.10), channel_id=1, source_target_pairs={{0,4},{4,0},{8,12},{12,8},{16,20},{20,16},{24,28},{28,24},{32,36},... | collective-permute-start | bytes 2113544 | tf_op jit(solution)/shard_map/ppermute | solution.py:74
  29.7 15.6 %collective-permute-start.11 = (bf16[4,176,128]{2,1,0:T(8,128)(2,1)S(1)}, bf16[4,176,128]{2,1,0:T(8,128)(2,1)S(1)}, u32[]{:S(2)}, u32[]{:S(2)}) collective-permute-start(bf16[4,176,128]{2,1,0:T(8,128)(2,1)S(1)} %pad_maximum_fusion.31), channel_id=1, source_target_pairs={{0,32},{4,36},{8,40},{12,44},{16,48},{20,52},{24,56},{28,60},{32,0... | collective-permute-start | bytes 540680 | tf_op jit(solution)/shard_map/ppermute | solution.py:74
  38.9 207.9 %copy-start.46 = (pred[256,2]{0,1:T(4,128)(4,1)}, pred[256,2]{0,1:T(4,128)(4,1)S(1)}, u32[]{:S(2)}) copy-start(pred[256,2]{0,1:T(4,128)(4,1)S(1)} %broadcast_in_dim.631) | copy-start | bytes 1540
  39.7 143.6 %copy-start.48 = (pred[256,2]{0,1:T(4,128)(4,1)}, pred[256,2]{0,1:T(4,128)(4,1)S(1)}, u32[]{:S(2)}) copy-start(pred[256,2]{0,1:T(4,128)(4,1)S(1)} %broadcast_in_dim.625) | copy-start | bytes 1540
  45.3 11.3 %collective-permute-start.12 = (bf16[8,176,128]{2,1,0:T(8,128)(2,1)S(1)}, bf16[8,176,128]{2,1,0:T(8,128)(2,1)S(1)}, u32[]{:S(2)}, u32[]{:S(2)}) collective-permute-start(bf16[8,176,128]{2,1,0:T(8,128)(2,1)S(1)} %pad_maximum_fusion.24), channel_id=1, source_target_pairs={{0,16},{4,20},{8,24},{12,28},{16,0},{20,4},{24,8},{28,12},{32,48},... | collective-permute-start | bytes 1081352 | tf_op jit(solution)/shard_map/ppermute | solution.py:74
  48.0 23.6 %collective-permute-start.2 = (bf16[4,352,128]{2,1,0:T(8,128)(2,1)S(1)}, bf16[4,352,128]{2,1,0:T(8,128)(2,1)S(1)}, u32[]{:S(2)}, u32[]{:S(2)}) collective-permute-start(bf16[4,352,128]{2,1,0:T(8,128)(2,1)S(1)} %pad_maximum_fusion.23), channel_id=1, source_target_pairs={{0,32},{4,36},{8,40},{12,44},{16,48},{20,52},{24,56},{28,60},{32,0... | collective-permute-start | bytes 1081352 | tf_op jit(solution)/shard_map/ppermute | solution.py:74
  57.4 10.5 %collective-permute-start.15 = (bf16[16,48,128]{2,1,0:T(8,128)(2,1)S(1)}, bf16[16,48,128]{2,1,0:T(8,128)(2,1)S(1)}, u32[]{:S(2)}, u32[]{:S(2)}) collective-permute-start(bf16[16,48,128]{2,1,0:T(8,128)(2,1)S(1)} %pad_maximum_fusion.30), channel_id=1, source_target_pairs={{0,128},{4,132},{8,136},{12,140},{16,144},{20,148},{24,152},{28,15... | collective-permute-start | bytes 589832 | tf_op jit(solution)/shard_map/ppermute | solution.py:74
  67.9 10.1 %collective-permute-start.16 = (bf16[32,48,128]{2,1,0:T(8,128)(2,1)S(1)}, bf16[32,48,128]{2,1,0:T(8,128)(2,1)S(1)}, u32[]{:S(2)}, u32[]{:S(2)}) collective-permute-start(bf16[32,48,128]{2,1,0:T(8,128)(2,1)S(1)} %pad_maximum_fusion.22), channel_id=1, source_target_pairs={{0,64},{4,68},{8,72},{12,76},{16,80},{20,84},{24,88},{28,92},{32,9... | collective-permute-start | bytes 1179656 | tf_op jit(solution)/shard_map/ppermute | solution.py:74
  71.7 17.7 %collective-permute-start.3 = (bf16[8,352,128]{2,1,0:T(8,128)(2,1)S(1)}, bf16[8,352,128]{2,1,0:T(8,128)(2,1)S(1)}, u32[]{:S(2)}, u32[]{:S(2)}) collective-permute-start(bf16[8,352,128]{2,1,0:T(8,128)(2,1)S(1)} %pad_maximum_fusion.8), channel_id=1, source_target_pairs={{0,16},{4,20},{8,24},{12,28},{16,0},{20,4},{24,8},{28,12},{32,48},... | collective-permute-start | bytes 2162696 | tf_op jit(solution)/shard_map/ppermute | solution.py:74
  78.1 17.3 %collective-permute-start.19 = (bf16[64,16,128]{2,1,0:T(8,128)(2,1)S(1)}, bf16[64,16,128]{2,1,0:T(8,128)(2,1)S(1)}, u32[]{:S(2)}, u32[]{:S(2)}) collective-permute-start(bf16[64,16,128]{2,1,0:T(8,128)(2,1)S(1)} %pad_maximum_fusion.27), channel_id=1, source_target_pairs={{256,0},{260,4},{264,8},{268,12},{272,16},{276,20},{280,24},{284,2... | collective-permute-start | bytes 786440 | tf_op jit(solution)/shard_map/ppermute | solution.py:74
  89.4 19.1 %collective-permute-start.4 = (bf16[16,96,128]{2,1,0:T(8,128)(2,1)S(1)}, bf16[16,96,128]{2,1,0:T(8,128)(2,1)S(1)}, u32[]{:S(2)}, u32[]{:S(2)}) collective-permute-start(bf16[16,96,128]{2,1,0:T(8,128)(2,1)S(1)} %pad_maximum_fusion.20), channel_id=1, source_target_pairs={{0,128},{4,132},{8,136},{12,140},{16,144},{20,148},{24,152},{28,15... | collective-permute-start | bytes 1179656 | tf_op jit(solution)/shard_map/ppermute | solution.py:74
  109.4 21.7 %collective-permute-start.5 = (bf16[32,96,128]{2,1,0:T(8,128)(2,1)}, bf16[32,96,128]{2,1,0:T(8,128)(2,1)}, u32[]{:S(2)}, u32[]{:S(2)}) collective-permute-start(bf16[32,96,128]{2,1,0:T(8,128)(2,1)} %pad_maximum_fusion.5), channel_id=1, source_target_pairs={{0,64},{4,68},{8,72},{12,76},{16,80},{20,84},{24,88},{28,92},{32,9... | collective-permute-start | bytes 2359304 | tf_op jit(solution)/shard_map/ppermute | solution.py:74
  133.0 30.1 %collective-permute-start.6 = (bf16[64,32,128]{2,1,0:T(8,128)(2,1)}, bf16[64,32,128]{2,1,0:T(8,128)(2,1)}, u32[]{:S(2)}, u32[]{:S(2)}) collective-permute-start(bf16[64,32,128]{2,1,0:T(8,128)(2,1)} %pad_maximum_fusion.17), channel_id=1, source_target_pairs={{0,256},{4,260},{8,264},{12,268},{16,272},{20,276},{24,280},{28,28... | collective-permute-start | bytes 1572872 | tf_op jit(solution)/shard_map/ppermute | solution.py:74
  226.3 7.6 %collective-permute-start.9 = (bf16[1,768,128]{2,1,0:T(8,128)(2,1)S(1)}, bf16[1,768,128]{2,1,0:T(8,128)(2,1)S(1)}, u32[]{:S(2)}, u32[]{:S(2)}) collective-permute-start(bf16[1,768,128]{2,1,0:T(8,128)(2,1)S(1)} %bitcast.334), channel_id=1, source_target_pairs={{0,8},{4,12},{8,0},{12,4},{16,24},{20,28},{24,16},{28,20},{32,40},... | collective-permute-start | bytes 589832 | tf_op jit(solution)/shard_map/ppermute | solution.py:74
  235.3 14.4 %collective-permute-start.10 = (bf16[2,768,128]{2,1,0:T(8,128)(2,1)}, bf16[2,768,128]{2,1,0:T(8,128)(2,1)S(1)}, u32[]{:S(2)}, u32[]{:S(2)}) collective-permute-start(bf16[2,768,128]{2,1,0:T(8,128)(2,1)} %pad_maximum_fusion.21), channel_id=1, source_target_pairs={{0,4},{4,0},{8,12},{12,8},{16,20},{20,16},{24,28},{28,24},{32,36},... | collective-permute-start | bytes 1179656 | tf_op jit(solution)/shard_map/ppermute | solution.py:74
  251.4 18.6 %collective-permute-start.13 = (bf16[4,224,128]{2,1,0:T(8,128)(2,1)S(1)}, bf16[4,224,128]{2,1,0:T(8,128)(2,1)S(1)}, u32[]{:S(2)}, u32[]{:S(2)}) collective-permute-start(bf16[4,224,128]{2,1,0:T(8,128)(2,1)S(1)} %pad_maximum_fusion.29), channel_id=1, source_target_pairs={{0,32},{4,36},{8,40},{12,44},{16,48},{20,52},{24,56},{28,60},{32,0... | collective-permute-start | bytes 688136 | tf_op jit(solution)/shard_map/ppermute | solution.py:74
  270.0 15.8 %collective-permute-start.14 = (bf16[8,224,128]{2,1,0:T(8,128)(2,1)S(1)}, bf16[8,224,128]{2,1,0:T(8,128)(2,1)S(1)}, u32[]{:S(2)}, u32[]{:S(2)}) collective-permute-start(bf16[8,224,128]{2,1,0:T(8,128)(2,1)S(1)} %pad_maximum_fusion.19), channel_id=1, source_target_pairs={{0,16},{4,20},{8,24},{12,28},{16,0},{20,4},{24,8},{28,12},{32,48},... | collective-permute-start | bytes 1376264 | tf_op jit(solution)/shard_map/ppermute | solution.py:74
  285.9 15.5 %collective-permute-start.17 = (bf16[16,80,128]{2,1,0:T(8,128)(2,1)S(1)}, bf16[16,80,128]{2,1,0:T(8,128)(2,1)}, u32[]{:S(2)}, u32[]{:S(2)}) collective-permute-start(bf16[16,80,128]{2,1,0:T(8,128)(2,1)S(1)} %pad_maximum_fusion.26), channel_id=1, source_target_pairs={{0,128},{4,132},{8,136},{12,140},{16,144},{20,148},{24,152},{28,15... | collective-permute-start | bytes 983048 | tf_op jit(solution)/shard_map/ppermute | solution.py:74
  303.3 18.2 %collective-permute-start.18 = (bf16[32,80,128]{2,1,0:T(8,128)(2,1)}, bf16[32,80,128]{2,1,0:T(8,128)(2,1)}, u32[]{:S(2)}, u32[]{:S(2)}) collective-permute-start(bf16[32,80,128]{2,1,0:T(8,128)(2,1)} %pad_maximum_fusion.12), channel_id=1, source_target_pairs={{0,64},{4,68},{8,72},{12,76},{16,80},{20,84},{24,88},{28,92},{32,9... | collective-permute-start | bytes 1966088 | tf_op jit(solution)/shard_map/ppermute | solution.py:74
  323.6 29.9 %collective-permute-start.20 = (bf16[64,32,128]{2,1,0:T(8,128)(2,1)}, bf16[64,32,128]{2,1,0:T(8,128)(2,1)}, u32[]{:S(2)}, u32[]{:S(2)}) collective-permute-start(bf16[64,32,128]{2,1,0:T(8,128)(2,1)} %get-tuple-element.33), channel_id=1, source_target_pairs={{256,0},{260,4},{264,8},{268,12},{272,16},{276,20},{280,24},{284,2... | collective-permute-start | bytes 1572872 | tf_op jit(solution)/shard_map/ppermute | solution.py:74
  (87 other events, 970.4 us)
